TPU v7x, 32 devices: a whole 2x2x4 slice. The times are simulated.
32 devices in a mesh: freq: 2 (over y), gx: 4 (over z), gy: 2 (over x), col: 2 (over core).
Axes of the slice: x: 2, y: 2, z: 4, core: 2. Of those that a mesh axis runs over, the one named last changes fastest.
Arguments:
- source: bfloat16 [12, 64, 32, 256], P('freq', 'gx', 'gy', 'col'), parts along dimension 0, may hold values from -6 to 6
- warm: bfloat16 [12, 64, 32, 256], P('freq', 'gx', 'gy', 'col'), parts along dimension 0, may hold values from -2.1 to 2.6
- forward: bfloat16 [12, 64, 32, 256], P('freq', 'gx', 'gy', 'col'), parts along dimension 0, may hold values from -6 to 6
- density: bfloat16 [64, 32, 256], P('gx', 'gy', 'col'), may hold values from 1 to 3
- material_map: int32 [8, 4, 8], P('gx', 'gy', 'col'), may hold values from 0 to 7
- material_table: float32 [8, 2], replicated, may hold values from 0.5 to 2
- iface_cells: int32 [16, 256], P(('gx', 'gy', 'col')), may hold values from 0 to 32767, as said below
- impedance: float32 [2, 3], replicated, may hold values from 2 to 8
- omega2: float32 [2], P('freq'), parts along dimension 0, may hold values from 0.5 to 1
Outputs:
- adjoint: float32 [12, 64, 32, 256], P('freq', 'gx', 'gy', 'col'), parts along dimension 0
- coarse_gradient: float32 [32, 8], P('freq'), parts along dimension 0
There are 2 independent parts, one for each index of `freq`. A program takes and returns all parts, laid end to end along the dimension named above; an argument that names none is the same for every part. Nothing has to cross between parts.
Inputs may be any that keep to these rules, and one draw needn't show every extreme that they name: `iface_cells`: each row's entries are distinct, rising, and within the tile of 16 x 16 x 128 cells; row r belongs to the device of that index along gx, gy and col together.
All inputs are finite; a program needn't handle non-finite values.
Results may differ from a plain program's by a relative error of at most 0.0003.
Values may be sent and summed in bfloat16 or wider, within the bound.
No kernel may reach another device: no remote copies, remote signals or barrier semaphores. Data moves between devices by JAX's collectives and lax.ppermute only.
A program may use at most 64 MiB of HBM per device.

v0:
```python
import jax
import jax.numpy as jnp
from jax import lax
from jax.sharding import PartitionSpec as P

DAMPING = 0.5
RELAXATION = 0.6


def with_halo(array, sides, width):
    for axis, dim in sides:
        peers, length = (lax.axis_size(axis), array.shape[dim])
        up = [(i, (i + 1) % peers) for i in range(peers - 1)]
        down = [(j, i) for i, j in up]
        last = lax.slice_in_dim(array, length - width, length, axis=dim)
        initial = lax.slice_in_dim(array, 0, width, axis=dim)
        before = lax.ppermute(last, axis, up)
        after = lax.ppermute(initial, axis, down)
        array = jnp.concatenate([before, array, after], axis=dim)
    return array


def window(padded, offset):
    size_x = padded.shape[1] - 2
    size_y = padded.shape[2] - 2
    size_z = padded.shape[3] - 2
    return padded[
        :,
        1 + offset[0] : 1 + offset[0] + size_x,
        1 + offset[1] : 1 + offset[1] + size_y,
        1 + offset[2] : 1 + offset[2] + size_z,
    ]


def navier(padded, lame_first, shear):
    units = ((1, 0, 0), (0, 1, 0), (0, 0, 1))
    centre = window(padded, (0, 0, 0))
    second = []
    for axis_d in range(3):
        ahead = units[axis_d]
        behind = tuple((-value for value in ahead))
        second.append(window(padded, ahead) + window(padded, behind) - 2.0 * centre)
    laplace = second[0] + second[1] + second[2]
    result = []
    for part_index in range(2):
        for component in range(3):
            channel = part_index * 3 + component
            divergence = second[component][channel]
            for other_axis in range(3):
                if other_axis != component:
                    source_channel = part_index * 3 + other_axis
                    single = padded[source_channel : source_channel + 1]
                    first_unit = units[component]
                    other_unit = units[other_axis]
                    plus_plus = tuple((first_unit[k] + other_unit[k] for k in range(3)))
                    plus_minus = tuple((first_unit[k] - other_unit[k] for k in range(3)))
                    minus_plus = tuple((-first_unit[k] + other_unit[k] for k in range(3)))
                    minus_minus = tuple((-first_unit[k] - other_unit[k] for k in range(3)))
                    mixed = (
                        window(single, plus_plus)
                        - window(single, plus_minus)
                        - window(single, minus_plus)
                        + window(single, minus_minus)
                    )
                    divergence = divergence + 0.25 * mixed[0]
            result.append(shear * laplace[channel] + (lame_first + shear) * divergence)
    return jnp.stack(result)


def sweep(padded, lame_first, shear, density, mask, source, mean_field, omega_sq, impedance):
    field = window(padded, (0, 0, 0))
    elastic = navier(padded, lame_first, shear)
    real_part = field[:3]
    imag_part = field[3:]
    mean_real = mean_field[:3][:, None, None, None]
    mean_imag = mean_field[3:][:, None, None, None]
    imp_real = impedance[0][:, None, None, None]
    imp_imag = impedance[1][:, None, None, None]
    inertia = omega_sq * density
    diff_real = real_part - mean_real
    diff_imag = imag_part - mean_imag
    apply_real = (
        -elastic[:3]
        - inertia * (real_part - DAMPING * imag_part)
        + mask * (imp_real * diff_real - imp_imag * diff_imag)
    )
    apply_imag = (
        -elastic[3:]
        - inertia * (imag_part + DAMPING * real_part)
        + mask * (imp_real * diff_imag + imp_imag * diff_real)
    )
    resid_real = source[:3] - apply_real
    resid_imag = source[3:] - apply_imag
    diag_real = 8.0 * shear + 2.0 * lame_first - inertia + mask * imp_real
    diag_imag = -DAMPING * inertia + mask * imp_imag
    modulus = diag_real * diag_real + diag_imag * diag_imag
    new_real = real_part + RELAXATION * (resid_real * diag_real + resid_imag * diag_imag) / modulus
    new_imag = imag_part + RELAXATION * (resid_imag * diag_real - resid_real * diag_imag) / modulus
    return jnp.concatenate([new_real, new_imag], 0)


def expand(blocks):
    blocks_x, blocks_y, blocks_z = blocks.shape
    spread = jnp.broadcast_to(
        blocks[:, None, :, None, :, None], (blocks_x, 8, blocks_y, 8, blocks_z, 32)
    )
    return spread.reshape(blocks_x * 8, blocks_y * 8, blocks_z * 32)


def material(block_ids, table):
    lame_first = jnp.zeros(block_ids.shape, jnp.float32)
    shear = jnp.zeros(block_ids.shape, jnp.float32)
    for entry in range(table.shape[0]):
        chosen = block_ids == entry
        lame_first = jnp.where(chosen, table[entry, 0], lame_first)
        shear = jnp.where(chosen, table[entry, 1], shear)
    return (lame_first, shear)


def foundation(field, mask, count):
    total = lax.psum(jnp.sum(mask * field, axis=(1, 2, 3)), ("gx", "gy", "col"))
    return total / count


def shards(
    source, warm, forward, density, material_map, material_table, iface_cells, impedance, omega2
):
    omega_sq = omega2[0]
    tile_shape = density.shape
    tile_cells = tile_shape[0] * tile_shape[1] * tile_shape[2]
    mask = jnp.zeros((tile_cells,), jnp.float32).at[iface_cells[0]].set(1.0).reshape(tile_shape)
    block_ids = expand(material_map)
    lame_first, shear = material(block_ids, material_table)
    density_cells = density.astype(jnp.float32)
    source_cells = source.astype(jnp.float32)
    group_size = lax.axis_size("gx") * lax.axis_size("gy") * lax.axis_size("col")
    count = jnp.float32(group_size * iface_cells.shape[1])
    field = warm.astype(jnp.float32)
    for sweep_index in range(2):
        mean_field = foundation(field, mask, count)
        padded = with_halo(field, (("gx", 1), ("gy", 2), ("col", 3)), 1)
        field = sweep(
            padded,
            lame_first,
            shear,
            density_cells,
            mask,
            source_cells,
            mean_field,
            omega_sq,
            impedance,
        )
    forward_cells = forward.astype(jnp.float32)
    correlation = (
        field[:3] * forward_cells[:3]
        - field[3:] * forward_cells[3:]
        - DAMPING * (field[:3] * forward_cells[3:] + field[3:] * forward_cells[:3])
    )
    cell_terms = -omega_sq * jnp.sum(correlation, axis=0)
    coarse_x = tile_shape[0] // 4
    coarse_y = tile_shape[1] // 4
    local_sums = cell_terms.reshape(coarse_x, 4, coarse_y, 4, tile_shape[2]).sum(axis=(1, 3, 4))
    paired = lax.psum(local_sums, "col")
    gathered = lax.all_gather(paired[None], ("gx", "gy"), axis=0, tiled=True)
    grid_sums = gathered.reshape(lax.axis_size("gx"), lax.axis_size("gy"), coarse_x, coarse_y)
    coarse = (
        grid_sums.transpose(0, 2, 1, 3).reshape(
            lax.axis_size("gx") * coarse_x, lax.axis_size("gy") * coarse_y
        )
        / 64.0
    )
    return (field, coarse)


def solution(mesh):
    in_specs = (
        P("freq", "gx", "gy", "col"),
        P("freq", "gx", "gy", "col"),
        P("freq", "gx", "gy", "col"),
        P("gx", "gy", "col"),
        P("gx", "gy", "col"),
        P(),
        P(("gx", "gy", "col"), None),
        P(),
        P("freq"),
    )
    out_specs = (P("freq", "gx", "gy", "col"), P("freq", None))
    return jax.shard_map(shards, mesh=mesh, in_specs=in_specs, out_specs=out_specs, check_vma=False)
```

profile of v0, /device:TPU:0, one launch (start us, length us, event | category | flops | bytes accessed | tf_op | source)
XLA Modules:
  0.0 208.3 jit_solution(2462226845284078183)
XLA Ops:
  0.6 0.8 fusion.107
  1.4 1.3 collective-permute-start
  2.7 5.6 %collective-permute-start.1 = (f32[6,1,16,128]{3,2,1,0:T(8,128)S(1)}, f32[6,1,16,128]{3,2,1,0:T(8,128)S(1)}, u32[]{:S(2)}, u32[]{:S(2)}) collective-permute-start(f32[6,1,16,128]{3,2,1,0:T(8,128)S(1)} %get-tuple-element.40), channel_id=1, source_target_pairs={{0,4},{4,8},{8,12},{1,5},{5,9},{9,13},{2,6},{6,10},{10,14},{3,7},{... | collective-permute-start | bytes 147464 | tf_op jit(solution)/shard_map/ppermute | solution.py:17
  8.3 2.0 fusion.108
  10.3 0.7 broadcast_compare_fusion.7
  11.0 1.9 broadcast_select_fusion
  12.9 4.6 %select_select_fusion.1 = f32[2,8,2,8,4,32]{5,4,3,2,1,0:T(4,128)S(1)} fusion(f32[]{:T(128)} %bitcast, f32[]{:T(128)} %bitcast.1, f32[]{:T(128)} %bitcast.2, f32[]{:T(128)} %bitcast.3, f32[]{:T(128)} %bitcast.4, f32[2,2,4]{2,1,0:T(2,128)S(1)} %get-tuple-element.46, f32[]{:T(128)} %bitcast.6, f32[]{:T(128)} %bitcast.5, ...), kind=kLoop, calls=%fused_computation.41 | loop fusion | flops 229376 | bytes 131276 | tf_op jit(solution)/shard_map/jit(_where)/select_n | solution.py:116
  17.4 4.5 %select_select_fusion = f32[2,8,2,8,4,32]{5,4,3,2,1,0:T(4,128)S(1)} fusion(f32[]{:T(128)} %bitcast.8, f32[]{:T(128)} %bitcast.9, f32[]{:T(128)} %bitcast.10, f32[]{:T(128)} %bitcast.11, f32[]{:T(128)} %bitcast.12, f32[2,2,4]{2,1,0:T(2,128)S(1)} %get-tuple-element.45, f32[]{:T(128)} %bitcast.14, f32[]{:T(128)} %bitcast.13, ...), kind=kLoop, calls=%fused_computation.40 | loop fusion | flops 229376 | bytes 131276 | tf_op jit(solution)/shard_map/jit(_where)/select_n | solution.py:115
  22.0 8.9 %multiply_add_fusion = f32[2,8,2,8,4,32]{5,4,3,2,1,0:T(4,128)S(1)} fusion(f32[2,2,4]{2,1,0:T(2,128)S(1)} %get-tuple-element.46, f32[]{:T(128)} %bitcast.6, pred[2,2,4]{2,1,0:T(4,128)(4,1)S(1)} %get-tuple-element.53, f32[]{:T(128)} %bitcast.5, pred[2,2,4]{2,1,0:T(4,128)(4,1)S(1)} %get-tuple-element.48, f32[]{:T(128)} %bitcast.4, ...), kind=kLoop, calls=%fused_computation.39 | loop fusion | flops 557056 | bytes 131368 | tf_op jit(solution)/shard_map/add | solution.py:94
  31.8 0.8 convert_multiply_fusion
  32.8 1.3 collective-permute-start.2
  34.1 5.8 %collective-permute-start.3 = (f32[6,18,1,128]{3,2,1,0:T(1,128)S(1)}, f32[6,18,1,128]{3,2,1,0:T(1,128)}, u32[]{:S(2)}, u32[]{:S(2)}) collective-permute-start(f32[6,18,1,128]{3,2,1,0:T(1,128)S(1)} %get-tuple-element.34), channel_id=1, source_target_pairs={{0,2},{1,3},{4,6},{5,7},{8,10},{9,11},{12,14},{13,15},{16,18},{17,... | collective-permute-start | bytes 165896 | tf_op jit(solution)/shard_map/ppermute | solution.py:17
  39.9 0.9 reshape.313
  40.8 0.9 reshape.315
  41.7 1.0 convert_element_type.13
  42.7 2.0 scatter_custom_fusion
  44.7 1.0 pad_maximum_fusion.3
  45.8 0.4 fusion.106
  46.2 1.6 copy.44
  47.8 1.3 collective-permute-start.4
  49.1 0.9 copy.46
  50.0 3.6 %collective-permute-start.5 = (f32[6,18,18,1]{2,1,3,0:T(8,128)S(1)}, f32[6,18,18,1]{2,1,3,0:T(8,128)}, u32[]{:S(2)}, u32[]{:S(2)}) collective-permute-start(f32[6,18,18,1]{2,1,3,0:T(8,128)S(1)} %copy.46), channel_id=1, source_target_pairs={{0,1},{2,3},{4,5},{6,7},{8,9},{10,11},{12,13},{14,15},{16,17},{18,... | collective-permute-start | bytes 23336 | tf_op jit(solution)/shard_map/ppermute | solution.py:17
  53.7 2.6 %pad_maximum_fusion.2 = (f32[6,18,17,128]{3,2,1,0:T(8,128)}, f32[6,18,17,128]{3,2,1,0:T(8,128)}) fusion(f32[6,18,1,128]{3,2,1,0:T(1,128)} %collective-permute-done.2, f32[6,1,16,128]{3,2,1,0:T(8,128)S(1)} %collective-permute-done, f32[6,16,16,128]{3,2,1,0:T(8,128)S(1)} %convert_element_type.12, f32[6,1,16,128]{3,2,1,0:T(8,128)S(1)} %collective-permute-done.1, ...), kind=kLoop, calls=%fused_computation.5 | loop fusion | flops 1410048 | bytes 2875392 | tf_op jit(solution)/shard_map/concatenate | solution.py:19
  56.2 0.8 copy.45
  57.0 1.7 copy.47
  58.7 3.1 %pad_maximum_fusion = (f32[6,18,18,129]{3,2,1,0:T(8,128)S(1)}, f32[6,18,18,129]{3,2,1,0:T(8,128)S(1)}) fusion(f32[6,18,18,1]{3,2,1,0:T(8,128)S(1)} %copy.45, f32[6,18,1,128]{3,2,1,0:T(1,128)} %collective-permute-done.2, f32[6,1,16,128]{3,2,1,0:T(8,128)S(1)} %collective-permute-done, f32[6,16,16,128]{3,2,1,0:T(8,128)S(1)} %convert_element_type.12, ...), kind=kLoop, calls=%fused_computation.1 | loop fusion | flops 2507760 | bytes 3017088 | tf_op jit(solution)/shard_map/concatenate | solution.py:19
  61.8 2.3 %add_add_fusion.1 = (f32[6,16,16,128]{3,2,1,0:T(8,128)}, f32[6,16,16,128]{3,2,1,0:T(8,128)}, f32[6,16,16,128]{3,2,1,0:T(8,128)}, f32[6,16,16,128]{3,2,1,0:T(8,128)}, f32[6]{0:T(128)S(1)}) fusion(bf16[6,16,16,128]{3,2,1,0:T(8,128)(2,1)S(1)} %copy-done.28, f32[6,18,17,128]{3,2,1,0:T(8,128)S(1)} %copy-done.17, f32[6,18,17,128]{3,2,1,0:T(8,128)S(1)} %copy-done.16, ...), kind=kLoop, calls=%fused_computation.38 | loop fusion | flops 2949114 | bytes 7700504 | tf_op jit(solution)/shard_map/add | solution.py:43
  64.2 29.5 %psum.21 = f32[6]{0:T(128)S(1)} all-reduce(f32[6]{0:T(128)S(1)} %get-tuple-element.39), channel_id=1, replica_groups=mesh['freq'=2,'gx'=4,'gy'=2,'col'=2] {'gx','gy','col'}, use_global_device_ids=true, to_apply=%region_2.3 | all-reduce | flops 6 | bytes 48 | tf_op jit(solution)/shard_map/psum | solution.py:121
  93.7 1.6 fusion.71
  95.4 1.4 fusion.89
  96.8 1.4 fusion.83
  98.3 1.4 fusion.65
  99.7 1.7 fusion.77
  101.5 1.7 fusion.59
  103.3 0.5 divide_add_fusion.3
  104.1 1.4 collective-permute-start.6
  105.5 4.5 %collective-permute-start.7 = (f32[6,1,16,128]{3,2,1,0:T(8,128)S(1)}, f32[6,1,16,128]{3,2,1,0:T(8,128)S(1)}, u32[]{:S(2)}, u32[]{:S(2)}) collective-permute-start(f32[6,1,16,128]{3,2,1,0:T(8,128)S(1)} %get-tuple-element.37), channel_id=1, source_target_pairs={{0,4},{4,8},{8,12},{1,5},{5,9},{9,13},{2,6},{6,10},{10,14},{3,7},{... | collective-permute-start | bytes 147464 | tf_op jit(solution)/shard_map/ppermute | solution.py:17
  110.2 1.6 collective-permute-done.7
  111.9 1.3 collective-permute-start.8
  113.2 4.7 %collective-permute-start.9 = (f32[6,18,1,128]{3,2,1,0:T(1,128)S(1)}, f32[6,18,1,128]{3,2,1,0:T(1,128)S(1)}, u32[]{:S(2)}, u32[]{:S(2)}) collective-permute-start(f32[6,18,1,128]{3,2,1,0:T(1,128)S(1)} %get-tuple-element.30), channel_id=1, source_target_pairs={{0,2},{1,3},{4,6},{5,7},{8,10},{9,11},{12,14},{13,15},{16,18},{17,... | collective-permute-start | bytes 165896 | tf_op jit(solution)/shard_map/ppermute | solution.py:17
  118.0 1.0 convert_element_type.15
  118.9 0.6 collective-permute-done.9
  119.6 0.6 copy-done.13
  120.8 1.6 copy.48
  122.4 1.4 collective-permute-start.10
  123.8 0.9 copy.50
  124.8 3.6 %collective-permute-start.11 = (f32[6,18,18,1]{2,1,3,0:T(8,128)S(1)}, f32[6,18,18,1]{2,1,3,0:T(8,128)}, u32[]{:S(2)}, u32[]{:S(2)}) collective-permute-start(f32[6,18,18,1]{2,1,3,0:T(8,128)S(1)} %copy.50), channel_id=1, source_target_pairs={{0,1},{2,3},{4,5},{6,7},{8,9},{10,11},{12,13},{14,15},{16,17},{18,... | collective-permute-start | bytes 23336 | tf_op jit(solution)/shard_map/ppermute | solution.py:17
  128.4 1.7 pad_maximum_fusion.4
  130.2 0.8 copy.49
  130.9 1.7 copy.51
  132.6 3.6 %pad_maximum_fusion.1 = (f32[6,18,18,129]{3,2,1,0:T(8,128)S(1)}, f32[6,18,18,129]{3,2,1,0:T(8,128)S(1)}) fusion(f32[6,18,18,1]{3,2,1,0:T(8,128)S(1)} %copy.49, f32[6,18,1,128]{3,2,1,0:T(1,128)} %copy-done.10, f32[6,1,16,128]{3,2,1,0:T(8,128)S(1)} %collective-permute-done.6, f32[3,16,16,128]{3,2,1,0:T(8,128)S(1)} %divide_add_fusion.2, ...), kind=kLoop, calls=%fused_computation.3 | loop fusion | flops 3009312 | bytes 3017088 | tf_op jit(solution)/shard_map/concatenate | solution.py:19
  136.3 2.3 %add_add_fusion = (f32[6,16,16,128]{3,2,1,0:T(8,128)}, f32[6,16,16,128]{3,2,1,0:T(8,128)}, f32[6,16,16,128]{3,2,1,0:T(8,128)}, f32[6,16,16,128]{3,2,1,0:T(8,128)}, f32[6]{0:T(128)S(1)}) fusion(f32[3,16,16,128]{3,2,1,0:T(8,128)S(1)} %divide_add_fusion.2, f32[3,16,16,128]{3,2,1,0:T(8,128)S(1)} %get-tuple-element.11, f32[6,18,17,128]{3,2,1,0:T(8,128)S(1)} %copy-done.19, ...), kind=kLoop, calls=%fused_computation.36 | loop fusion | flops 3145722 | bytes 7307288 | tf_op jit(solution)/shard_map/add | solution.py:43
  138.6 29.5 %psum.22 = f32[6]{0:T(128)S(1)} all-reduce(f32[6]{0:T(128)S(1)} %get-tuple-element.36), channel_id=1, replica_groups=mesh['freq'=2,'gx'=4,'gy'=2,'col'=2] {'gx','gy','col'}, use_global_device_ids=true, to_apply=%region_4.5 | all-reduce | flops 6 | bytes 48 | tf_op jit(solution)/shard_map/psum | solution.py:121
  168.1 1.6 fusion.53
  169.8 1.3 fusion.35
  171.0 1.3 fusion.47
  172.3 1.3 fusion.29
  173.6 1.6 fusion.41
  175.3 1.7 fusion.23
  177.0 0.7 subtract_reduce_fusion
  178.1 2.4 %psum.23 = f32[1,4,4]{2,1,0:T(4,128)S(1)} all-reduce(f32[1,4,4]{2,1,0:T(4,128)S(1)} %bitcast.39), channel_id=1, replica_groups=mesh['freq'=2,'gx'=4,'gy'=2,'col'=2] {'col'}, use_global_device_ids=true, to_apply=%region_8.9 | all-reduce | flops 16 | bytes 128 | tf_op jit(solution)/shard_map/psum | solution.py:163
  180.5 26.0 %all_gather.3 = f32[8,4,4]{2,1,0:T(4,128)S(1)} all-gather(f32[1,4,4]{2,1,0:T(4,128)S(1)} %psum.23), channel_id=1, replica_groups=mesh['freq'=2,'gx'=4,'gy'=2,'col'=2] {'gx','gy'}, dimensions={0}, use_global_device_ids=true | all-gather | bytes 576 | tf_op jit(solution)/shard_map/all_gather | solution.py:164
  206.7 0.7 div.40
  207.3 0.9 pad_maximum_fusion.13
  (101 shorter events, 2.3 us)
Async XLA Ops:
  0.6 31.2 %copy-start.33 = (bf16[16,16,128]{2,1,0:T(8,128)(2,1)S(1)}, bf16[16,16,128]{2,1,0:T(8,128)(2,1)}, u32[]{:S(2)}) copy-start(bf16[16,16,128]{2,1,0:T(8,128)(2,1)} %param.12) | copy-start | bytes 196612
  1.4 31.2 %collective-permute-start = (f32[6,1,16,128]{3,2,1,0:T(8,128)S(1)}, f32[6,1,16,128]{3,2,1,0:T(8,128)S(1)}, u32[]{:S(2)}, u32[]{:S(2)}) collective-permute-start(f32[6,1,16,128]{3,2,1,0:T(8,128)S(1)} %get-tuple-element.41), channel_id=1, source_target_pairs={{4,0},{8,4},{12,8},{5,1},{9,5},{13,9},{6,2},{10,6},{14,10},{7,3},{... | collective-permute-start | bytes 147464 | tf_op jit(solution)/shard_map/ppermute | solution.py:18
  2.7 30.0 %collective-permute-start.1 = (f32[6,1,16,128]{3,2,1,0:T(8,128)S(1)}, f32[6,1,16,128]{3,2,1,0:T(8,128)S(1)}, u32[]{:S(2)}, u32[]{:S(2)}) collective-permute-start(f32[6,1,16,128]{3,2,1,0:T(8,128)S(1)} %get-tuple-element.40), channel_id=1, source_target_pairs={{0,4},{4,8},{8,12},{1,5},{5,9},{9,13},{2,6},{6,10},{10,14},{3,7},{... | collective-permute-start | bytes 147464 | tf_op jit(solution)/shard_map/ppermute | solution.py:17
  12.9 19.7 %copy-start.34 = (s32[1,256]{1,0:T(1,128)S(1)}, s32[1,256]{1,0:T(1,128)}, u32[]{:S(2)}) copy-start(s32[1,256]{1,0:T(1,128)} %param.15) | copy-start | bytes 3076
  12.9 19.7 %copy-start.27 = (bf16[6,16,16,128]{3,2,1,0:T(8,128)(2,1)S(1)}, bf16[6,16,16,128]{3,2,1,0:T(8,128)(2,1)}, u32[]{:S(2)}) copy-start(bf16[6,16,16,128]{3,2,1,0:T(8,128)(2,1)} %param.10) | copy-start | bytes 1179652
  31.8 8.1 %copy-start.35 = (f32[2,3]{1,0:T(2,128)S(1)}, f32[2,3]{1,0:T(2,128)}, u32[]{:S(2)}) copy-start(f32[2,3]{1,0:T(2,128)} %param.16) | copy-start | bytes 76
  32.7 9.0 %copy-start.31 = (bf16[6,16,16,128]{3,2,1,0:T(8,128)(2,1)S(1)}, bf16[6,16,16,128]{3,2,1,0:T(8,128)(2,1)}, u32[]{:S(2)}) copy-start(bf16[6,16,16,128]{3,2,1,0:T(8,128)(2,1)} %param.9) | copy-start | bytes 1179652
  32.8 11.9 %collective-permute-start.2 = (f32[6,18,1,128]{3,2,1,0:T(1,128)S(1)}, f32[6,18,1,128]{3,2,1,0:T(1,128)}, u32[]{:S(2)}, u32[]{:S(2)}) collective-permute-start(f32[6,18,1,128]{3,2,1,0:T(1,128)S(1)} %get-tuple-element.35), channel_id=1, source_target_pairs={{2,0},{3,1},{6,4},{7,5},{10,8},{11,9},{14,12},{15,13},{18,16},{19,... | collective-permute-start | bytes 165896 | tf_op jit(solution)/shard_map/ppermute | solution.py:18
  34.1 10.6 %collective-permute-start.3 = (f32[6,18,1,128]{3,2,1,0:T(1,128)S(1)}, f32[6,18,1,128]{3,2,1,0:T(1,128)}, u32[]{:S(2)}, u32[]{:S(2)}) collective-permute-start(f32[6,18,1,128]{3,2,1,0:T(1,128)S(1)} %get-tuple-element.34), channel_id=1, source_target_pairs={{0,2},{1,3},{4,6},{5,7},{8,10},{9,11},{12,14},{13,15},{16,18},{17,... | collective-permute-start | bytes 165896 | tf_op jit(solution)/shard_map/ppermute | solution.py:17
  47.8 8.5 %collective-permute-start.4 = (f32[6,18,18,1]{2,1,3,0:T(8,128)}, f32[6,18,18,1]{2,1,3,0:T(8,128)S(1)}, u32[]{:S(2)}, u32[]{:S(2)}) collective-permute-start(f32[6,18,18,1]{2,1,3,0:T(8,128)} %copy.44), channel_id=1, source_target_pairs={{1,0},{3,2},{5,4},{7,6},{9,8},{11,10},{13,12},{15,14},{17,16},{19,... | collective-permute-start | bytes 23336 | tf_op jit(solution)/shard_map/ppermute | solution.py:18
  50.0 7.0 %collective-permute-start.5 = (f32[6,18,18,1]{2,1,3,0:T(8,128)S(1)}, f32[6,18,18,1]{2,1,3,0:T(8,128)}, u32[]{:S(2)}, u32[]{:S(2)}) collective-permute-start(f32[6,18,18,1]{2,1,3,0:T(8,128)S(1)} %copy.46), channel_id=1, source_target_pairs={{0,1},{2,3},{4,5},{6,7},{8,9},{10,11},{12,13},{14,15},{16,17},{18,... | collective-permute-start | bytes 23336 | tf_op jit(solution)/shard_map/ppermute | solution.py:17
  58.7 3.1 %copy-start.6 = (f32[32768]{0:T(1024)S(1)}, f32[32768]{0:T(1024)}, u32[]{:S(2)}) copy-start(f32[32768]{0:T(1024)} %scatter_custom_fusion) | copy-start | bytes 393220
  58.7 3.1 %copy-start.16 = (f32[6,18,17,128]{3,2,1,0:T(8,128)S(1)}, f32[6,18,17,128]{3,2,1,0:T(8,128)}, u32[]{:S(2)}) copy-start(f32[6,18,17,128]{3,2,1,0:T(8,128)} %get-tuple-element.32) | copy-start | bytes 2820100
  58.7 3.1 %copy-start.17 = (f32[6,18,17,128]{3,2,1,0:T(8,128)S(1)}, f32[6,18,17,128]{3,2,1,0:T(8,128)}, u32[]{:S(2)}) copy-start(f32[6,18,17,128]{3,2,1,0:T(8,128)} %get-tuple-element.33) | copy-start | bytes 2820100
  58.7 3.1 %copy-start.28 = (bf16[6,16,16,128]{3,2,1,0:T(8,128)(2,1)S(1)}, bf16[6,16,16,128]{3,2,1,0:T(8,128)(2,1)}, u32[]{:S(2)}) copy-start(bf16[6,16,16,128]{3,2,1,0:T(8,128)(2,1)} %param.10) | copy-start | bytes 1179652
  93.7 1.6 copy-start
  93.7 1.7 copy-start.20
  95.3 6.1 %copy-start.2 = (f32[1,16,16,128]{3,2,1,0:T(8,128)}, f32[1,16,16,128]{3,2,1,0:T(8,128)S(1)}, u32[]{:S(2)}) copy-start(f32[1,16,16,128]{3,2,1,0:T(8,128)S(1)} %get-tuple-element.15) | copy-start | bytes 393220
  101.4 1.8 copy-start.4
  101.4 1.8 copy-start.7
  101.5 1.8 copy-start.23
  101.5 1.8 copy-start.25
  101.5 1.8 copy-start.29
  104.1 13.9 %copy-start.32 = (bf16[6,16,16,128]{3,2,1,0:T(8,128)(2,1)S(1)}, bf16[6,16,16,128]{3,2,1,0:T(8,128)(2,1)}, u32[]{:S(2)}) copy-start(bf16[6,16,16,128]{3,2,1,0:T(8,128)(2,1)} %param.11) | copy-start | bytes 1179652
  104.1 6.1 %collective-permute-start.6 = (f32[6,1,16,128]{3,2,1,0:T(8,128)S(1)}, f32[6,1,16,128]{3,2,1,0:T(8,128)S(1)}, u32[]{:S(2)}, u32[]{:S(2)}) collective-permute-start(f32[6,1,16,128]{3,2,1,0:T(8,128)S(1)} %get-tuple-element.38), channel_id=1, source_target_pairs={{4,0},{8,4},{12,8},{5,1},{9,5},{13,9},{6,2},{10,6},{14,10},{7,3},{... | collective-permute-start | bytes 147464 | tf_op jit(solution)/shard_map/ppermute | solution.py:18
  105.5 6.3 %collective-permute-start.7 = (f32[6,1,16,128]{3,2,1,0:T(8,128)S(1)}, f32[6,1,16,128]{3,2,1,0:T(8,128)S(1)}, u32[]{:S(2)}, u32[]{:S(2)}) collective-permute-start(f32[6,1,16,128]{3,2,1,0:T(8,128)S(1)} %get-tuple-element.37), channel_id=1, source_target_pairs={{0,4},{4,8},{8,12},{1,5},{5,9},{9,13},{2,6},{6,10},{10,14},{3,7},{... | collective-permute-start | bytes 147464 | tf_op jit(solution)/shard_map/ppermute | solution.py:17
  111.9 7.0 %collective-permute-start.8 = (f32[6,18,1,128]{3,2,1,0:T(1,128)S(1)}, f32[6,18,1,128]{3,2,1,0:T(1,128)S(1)}, u32[]{:S(2)}, u32[]{:S(2)}) collective-permute-start(f32[6,18,1,128]{3,2,1,0:T(1,128)S(1)} %get-tuple-element.31), channel_id=1, source_target_pairs={{2,0},{3,1},{6,4},{7,5},{10,8},{11,9},{14,12},{15,13},{18,16},{19,... | collective-permute-start | bytes 165896 | tf_op jit(solution)/shard_map/ppermute | solution.py:18
  113.2 6.3 %collective-permute-start.9 = (f32[6,18,1,128]{3,2,1,0:T(1,128)S(1)}, f32[6,18,1,128]{3,2,1,0:T(1,128)S(1)}, u32[]{:S(2)}, u32[]{:S(2)}) collective-permute-start(f32[6,18,1,128]{3,2,1,0:T(1,128)S(1)} %get-tuple-element.30), channel_id=1, source_target_pairs={{0,2},{1,3},{4,6},{5,7},{8,10},{9,11},{12,14},{13,15},{16,18},{17,... | collective-permute-start | bytes 165896 | tf_op jit(solution)/shard_map/ppermute | solution.py:17
  118.9 0.6 copy-start.10
  119.6 0.6 copy-start.13
  122.4 6.0 %copy-start.11 = (f32[6,18,1,128]{3,2,1,0:T(1,128)S(1)}, f32[6,18,1,128]{3,2,1,0:T(1,128)}, u32[]{:S(2)}) copy-start(f32[6,18,1,128]{3,2,1,0:T(1,128)} %copy-done.10) | copy-start | bytes 165892
  122.4 6.0 %copy-start.14 = (f32[6,18,1,128]{3,2,1,0:T(1,128)S(1)}, f32[6,18,1,128]{3,2,1,0:T(1,128)}, u32[]{:S(2)}) copy-start(f32[6,18,1,128]{3,2,1,0:T(1,128)} %copy-done.13) | copy-start | bytes 165892
  122.4 7.8 %collective-permute-start.10 = (f32[6,18,18,1]{2,1,3,0:T(8,128)}, f32[6,18,18,1]{2,1,3,0:T(8,128)S(1)}, u32[]{:S(2)}, u32[]{:S(2)}) collective-permute-start(f32[6,18,18,1]{2,1,3,0:T(8,128)} %copy.48), channel_id=1, source_target_pairs={{1,0},{3,2},{5,4},{7,6},{9,8},{11,10},{13,12},{15,14},{17,16},{19,... | collective-permute-start | bytes 23336 | tf_op jit(solution)/shard_map/ppermute | solution.py:18
  124.8 6.2 %collective-permute-start.11 = (f32[6,18,18,1]{2,1,3,0:T(8,128)S(1)}, f32[6,18,18,1]{2,1,3,0:T(8,128)}, u32[]{:S(2)}, u32[]{:S(2)}) collective-permute-start(f32[6,18,18,1]{2,1,3,0:T(8,128)S(1)} %copy.50), channel_id=1, source_target_pairs={{0,1},{2,3},{4,5},{6,7},{8,9},{10,11},{12,13},{14,15},{16,17},{18,... | collective-permute-start | bytes 23336 | tf_op jit(solution)/shard_map/ppermute | solution.py:17
  132.6 3.7 %copy-start.8 = (f32[32768]{0:T(1024)S(1)}, f32[32768]{0:T(1024)}, u32[]{:S(2)}) copy-start(f32[32768]{0:T(1024)} %scatter_custom_fusion) | copy-start | bytes 393220
  132.6 3.7 %copy-start.18 = (f32[6,18,17,128]{3,2,1,0:T(8,128)S(1)}, f32[6,18,17,128]{3,2,1,0:T(8,128)}, u32[]{:S(2)}) copy-start(f32[6,18,17,128]{3,2,1,0:T(8,128)} %get-tuple-element.28) | copy-start | bytes 2820100
  132.6 3.7 %copy-start.19 = (f32[6,18,17,128]{3,2,1,0:T(8,128)S(1)}, f32[6,18,17,128]{3,2,1,0:T(8,128)}, u32[]{:S(2)}) copy-start(f32[6,18,17,128]{3,2,1,0:T(8,128)} %get-tuple-element.29) | copy-start | bytes 2820100
  168.1 1.6 copy-start.1
  168.1 1.6 copy-start.3
  168.1 1.6 copy-start.12
  168.1 1.6 copy-start.15
  168.1 1.6 copy-start.22
  175.2 1.8 copy-start.5
  175.2 1.8 copy-start.9
  175.2 1.8 copy-start.21
  175.2 1.8 copy-start.24
  175.3 1.8 copy-start.26
  175.3 1.8 copy-start.30
where the time goes:
time: 210 us; the launch traced here: 208 us
  blocking collectives  87.4 us (42%)
  other arithmetic  61.2 us (29%)
  starting transfers between devices  35.9 us (17%)
  local copies, waits for them, and re-layouts  19.4 us (9%)
  waiting for transfers between devices  2.4 us (1%)
    psum x2, blocking collectives, foundation(): total = lax.psum(jnp.sum(mask * field, axis=(1, 2, 3)), ('gx', 'gy', 'col'))  58.9 us
    ppermute x6, starting transfers between devices, with_halo(): before = lax.ppermute(last, axis, up)  27.9 us
    all_gather x1, blocking collectives, shards(): gathered = lax.all_gather(paired[None], ('gx', 'gy'), axis=0, tiled=True)  26 us
    add x12, other arithmetic, navier(): result.append(shear * laplace[channel] + (lame_first + shear) * divergence)  18.1 us
    concatenate x8, other arithmetic, with_halo(): array = jnp.concatenate([before, array, after], axis=dim)  12.4 us
    add x1, other arithmetic, sweep(): diag_real = 8.0 * shear + 2.0 * lame_first - inertia + mask * imp_real  8.89 us
    ppermute x6, starting transfers between devices, with_halo(): after = lax.ppermute(initial, axis, down)  7.99 us
    select_n x2, other arithmetic, material(): lame_first = jnp.where(chosen, table[entry, 0], lame_first)  6.44 us
  transfers between devices with their start and end apart: 12, of which 3 were waited for; matrix products, arithmetic and copies ran while one was open for 18% of the time, Pallas kernels for 0%

commit v1 on v0

--- a/solution.py
+++ b/solution.py
@@ -118,7 +118,7 @@
 
 
 def foundation(field, mask, count):
-    total = lax.psum(jnp.sum(mask * field, axis=(1, 2, 3)), ("gx", "gy", "col"))
+    total = lax.psum(lax.psum(jnp.sum(mask * field, axis=(1, 2, 3)), ("gy", "col")), "gx")
     return total / count
 
 

time: 210 us -> 185 us (0.88)
  blocking collectives: 87.4 us -> 61.5 us
    psum x2 -> x4, blocking collectives: 58.9 us -> 33.1 us  [the longest x2 21 us: foundation(): lax.psum(lax.psum(jnp.sum(mask * field, axis=(1, 2, 3)), ('gy', 'col')),...]
  transfers between devices with their start and end apart: 12 -> 12, of which waited for: 3 -> 3; matrix products, arithmetic and copies ran while one was open for 18% -> 20% of each run, Pallas kernels for 0% -> 0%
where the time goes in v1:
time: 185 us; the launch traced here: 183 us
  other arithmetic  62 us (34%)
  blocking collectives  61.5 us (33%)
  starting transfers between devices  35.9 us (19%)
  local copies, waits for them, and re-layouts  19.4 us (10%)
  waiting for transfers between devices  2.4 us (1%)
  between operations  1.98 us (1%)
    ppermute x6, starting transfers between devices, with_halo(): before = lax.ppermute(last, axis, up)  27.9 us
    all_gather x1, blocking collectives, shards(): gathered = lax.all_gather(paired[None], ('gx', 'gy'), axis=0, tiled=True)  26 us
    psum x2, blocking collectives, foundation(): lax.psum(lax.psum(jnp.sum(mask * field, axis=(1, 2, 3)), ('gy', 'col')),...  21 us
    add x12, other arithmetic, navier(): result.append(shear * laplace[channel] + (lame_first + shear) * divergence)  18.1 us
    concatenate x8, other arithmetic, with_halo(): array = jnp.concatenate([before, array, after], axis=dim)  12.4 us
    psum x2, blocking collectives, foundation(): lax.psum(jnp.sum(mask * field, axis=(1, 2, 3)), ('gy', 'col'))  12.1 us
    add x1, other arithmetic, sweep(): diag_real = 8.0 * shear + 2.0 * lame_first - inertia + mask * imp_real  8.78 us
    ppermute x6, starting transfers between devices, with_halo(): after = lax.ppermute(initial, axis, down)  7.99 us
  transfers between devices with their start and end apart: 12, of which 3 were waited for; matrix products, arithmetic and copies ran while one was open for 20% of the time, Pallas kernels for 0%

profile of v1, /device:TPU:0, one launch (start us, length us, event | category | flops | bytes accessed | tf_op | source)
XLA Modules:
  0.0 183.2 jit_solution(7849595298388787738)
XLA Ops:
  0.6 0.8 fusion.107
  1.4 1.3 collective-permute-start
  2.7 5.6 %collective-permute-start.1 = (f32[6,1,16,128]{3,2,1,0:T(8,128)S(1)}, f32[6,1,16,128]{3,2,1,0:T(8,128)S(1)}, u32[]{:S(2)}, u32[]{:S(2)}) collective-permute-start(f32[6,1,16,128]{3,2,1,0:T(8,128)S(1)} %get-tuple-element.40), channel_id=1, source_target_pairs={{0,4},{4,8},{8,12},{1,5},{5,9},{9,13},{2,6},{6,10},{10,14},{3,7},{... | collective-permute-start | bytes 147464 | tf_op jit(solution)/shard_map/ppermute | solution.py:17
  8.3 2.0 %fusion.108 = (f32[1,1]{0,1:T(1,128)}, f32[1,1]{0,1:T(1,128)}, f32[1,1]{0,1:T(1,128)}, f32[1,1]{0,1:T(1,128)}, f32[1,1]{0,1:T(1,128)}, /*index=5*/f32[1,1]{0,1:T...) fusion(f32[8,2]{0,1:T(2,128)} %param.14), kind=kLoop, calls=%fused_computation.256 | loop fusion | bytes 128 | tf_op jit(solution)/shard_map/slice | solution.py:115
  10.3 0.7 broadcast_compare_fusion.7
  11.0 2.0 %broadcast_select_fusion = (f32[2,2,4]{2,1,0:T(2,128)S(1)}, f32[2,2,4]{2,1,0:T(2,128)S(1)}) fusion(f32[]{:T(128)} %bitcast.15, s32[2,2,4]{2,1,0:T(2,128)} %param.13, f32[]{:T(128)} %bitcast.7), kind=kLoop, calls=%fused_computation.239 | loop fusion | flops 48 | bytes 200 | tf_op jit(solution)/shard_map/jit(_where)/select_n | solution.py:115
  12.9 4.4 %select_select_fusion.1 = f32[2,8,2,8,4,32]{5,4,3,2,1,0:T(4,128)S(1)} fusion(f32[]{:T(128)} %bitcast, f32[]{:T(128)} %bitcast.1, f32[]{:T(128)} %bitcast.2, f32[]{:T(128)} %bitcast.3, f32[]{:T(128)} %bitcast.4, f32[2,2,4]{2,1,0:T(2,128)S(1)} %get-tuple-element.46, f32[]{:T(128)} %bitcast.6, f32[]{:T(128)} %bitcast.5, ...), kind=kLoop, calls=%fused_computation.41 | loop fusion | flops 229376 | bytes 131276 | tf_op jit(solution)/shard_map/jit(_where)/select_n | solution.py:116
  17.4 4.6 %select_select_fusion = f32[2,8,2,8,4,32]{5,4,3,2,1,0:T(4,128)S(1)} fusion(f32[]{:T(128)} %bitcast.8, f32[]{:T(128)} %bitcast.9, f32[]{:T(128)} %bitcast.10, f32[]{:T(128)} %bitcast.11, f32[]{:T(128)} %bitcast.12, f32[2,2,4]{2,1,0:T(2,128)S(1)} %get-tuple-element.45, f32[]{:T(128)} %bitcast.14, f32[]{:T(128)} %bitcast.13, ...), kind=kLoop, calls=%fused_computation.40 | loop fusion | flops 229376 | bytes 131276 | tf_op jit(solution)/shard_map/jit(_where)/select_n | solution.py:115
  21.9 8.8 %multiply_add_fusion = f32[2,8,2,8,4,32]{5,4,3,2,1,0:T(4,128)S(1)} fusion(f32[2,2,4]{2,1,0:T(2,128)S(1)} %get-tuple-element.46, f32[]{:T(128)} %bitcast.6, pred[2,2,4]{2,1,0:T(4,128)(4,1)S(1)} %get-tuple-element.53, f32[]{:T(128)} %bitcast.5, pred[2,2,4]{2,1,0:T(4,128)(4,1)S(1)} %get-tuple-element.48, f32[]{:T(128)} %bitcast.4, ...), kind=kLoop, calls=%fused_computation.39 | loop fusion | flops 557056 | bytes 131368 | tf_op jit(solution)/shard_map/add | solution.py:94
  31.7 0.8 convert_multiply_fusion
  32.6 1.3 collective-permute-start.2
  33.9 5.8 %collective-permute-start.3 = (f32[6,18,1,128]{3,2,1,0:T(1,128)S(1)}, f32[6,18,1,128]{3,2,1,0:T(1,128)}, u32[]{:S(2)}, u32[]{:S(2)}) collective-permute-start(f32[6,18,1,128]{3,2,1,0:T(1,128)S(1)} %get-tuple-element.34), channel_id=1, source_target_pairs={{0,2},{1,3},{4,6},{5,7},{8,10},{9,11},{12,14},{13,15},{16,18},{17,... | collective-permute-start | bytes 165896 | tf_op jit(solution)/shard_map/ppermute | solution.py:17
  39.7 0.9 reshape.313
  40.6 0.9 reshape.315
  41.5 2.0 %scatter_custom_fusion = f32[32768]{0:T(1024)} fusion(s32[256]{0:T(256)S(1)} %bitcast.40, f32[256]{0:T(256)S(1)} %broadcast.754, f32[]{:T(128)} %constant.7.clone.1), kind=kCustom, calls=%fused_computation.225 | custom fusion | bytes 131076 | tf_op jit(solution)/shard_map/scatter | solution.py:131
  43.6 1.0 pad_maximum_fusion.3
  45.0 1.6 copy.44
  46.6 1.3 collective-permute-start.4
  47.9 0.9 copy.46
  48.8 3.7 %collective-permute-start.5 = (f32[6,18,18,1]{2,1,3,0:T(8,128)S(1)}, f32[6,18,18,1]{2,1,3,0:T(8,128)}, u32[]{:S(2)}, u32[]{:S(2)}) collective-permute-start(f32[6,18,18,1]{2,1,3,0:T(8,128)S(1)} %copy.46), channel_id=1, source_target_pairs={{0,1},{2,3},{4,5},{6,7},{8,9},{10,11},{12,13},{14,15},{16,17},{18,... | collective-permute-start | bytes 23336 | tf_op jit(solution)/shard_map/ppermute | solution.py:17
  52.5 2.6 %pad_maximum_fusion.2 = (f32[6,18,17,128]{3,2,1,0:T(8,128)}, f32[6,18,17,128]{3,2,1,0:T(8,128)}) fusion(f32[6,18,1,128]{3,2,1,0:T(1,128)} %collective-permute-done.2, f32[6,1,16,128]{3,2,1,0:T(8,128)S(1)} %collective-permute-done, f32[6,16,16,128]{3,2,1,0:T(8,128)S(1)} %convert_element_type.12, f32[6,1,16,128]{3,2,1,0:T(8,128)S(1)} %collective-permute-done.1, ...), kind=kLoop, calls=%fused_computation.5 | loop fusion | flops 1410048 | bytes 2875392 | tf_op jit(solution)/shard_map/concatenate | solution.py:19
  55.0 0.8 copy.45
  55.8 1.7 copy.47
  57.5 3.1 %pad_maximum_fusion = (f32[6,18,18,129]{3,2,1,0:T(8,128)S(1)}, f32[6,18,18,129]{3,2,1,0:T(8,128)S(1)}) fusion(f32[6,18,18,1]{3,2,1,0:T(8,128)S(1)} %copy.45, f32[6,18,1,128]{3,2,1,0:T(1,128)} %collective-permute-done.2, f32[6,1,16,128]{3,2,1,0:T(8,128)S(1)} %collective-permute-done, f32[6,16,16,128]{3,2,1,0:T(8,128)S(1)} %convert_element_type.12, ...), kind=kLoop, calls=%fused_computation.1 | loop fusion | flops 2507760 | bytes 3017088 | tf_op jit(solution)/shard_map/concatenate | solution.py:19
  60.6 2.3 %add_add_fusion.1 = (f32[6,16,16,128]{3,2,1,0:T(8,128)}, f32[6,16,16,128]{3,2,1,0:T(8,128)}, f32[6,16,16,128]{3,2,1,0:T(8,128)}, f32[6,16,16,128]{3,2,1,0:T(8,128)}, f32[6]{0:T(128)S(1)}) fusion(bf16[6,16,16,128]{3,2,1,0:T(8,128)(2,1)S(1)} %copy-done.28, f32[6,18,17,128]{3,2,1,0:T(8,128)S(1)} %copy-done.17, f32[6,18,17,128]{3,2,1,0:T(8,128)S(1)} %copy-done.16, ...), kind=kLoop, calls=%fused_computation.38 | loop fusion | flops 2949114 | bytes 7700504 | tf_op jit(solution)/shard_map/add | solution.py:43
  62.9 5.7 %psum.35 = f32[6]{0:T(128)S(1)} all-reduce(f32[6]{0:T(128)S(1)} %get-tuple-element.39), channel_id=1, replica_groups=mesh['freq'=2,'gx'=4,'gy'=2,'col'=2] {'gy','col'}, use_global_device_ids=true, to_apply=%region_2.3 | all-reduce | flops 6 | bytes 48 | tf_op jit(solution)/shard_map/psum | solution.py:121
  68.7 2.0 %convert_element_type.13 = f32[6,16,16,128]{3,2,1,0:T(8,128)} convert(bf16[6,16,16,128]{3,2,1,0:T(8,128)(2,1)} %param.9) | non-fusion elementwise | flops 196608 | bytes 1179648 | tf_op jit(solution)/shard_map/convert_element_type | solution.py:135
  70.7 10.3 %psum.36 = f32[6]{0:T(128)S(1)} all-reduce(f32[6]{0:T(128)S(1)} %psum.35), channel_id=1, replica_groups=mesh['freq'=2,'gx'=4,'gy'=2,'col'=2] {'gx'}, use_global_device_ids=true, to_apply=%region_3.4 | all-reduce | flops 6 | bytes 48 | tf_op jit(solution)/shard_map/psum | solution.py:121
  81.1 1.6 fusion.71
  82.8 1.4 fusion.89
  84.2 1.4 fusion.83
  85.7 1.4 fusion.65
  87.1 1.7 fusion.77
  88.9 1.7 fusion.59
  91.5 1.4 collective-permute-start.6
  93.0 4.5 %collective-permute-start.7 = (f32[6,1,16,128]{3,2,1,0:T(8,128)S(1)}, f32[6,1,16,128]{3,2,1,0:T(8,128)S(1)}, u32[]{:S(2)}, u32[]{:S(2)}) collective-permute-start(f32[6,1,16,128]{3,2,1,0:T(8,128)S(1)} %get-tuple-element.37), channel_id=1, source_target_pairs={{0,4},{4,8},{8,12},{1,5},{5,9},{9,13},{2,6},{6,10},{10,14},{3,7},{... | collective-permute-start | bytes 147464 | tf_op jit(solution)/shard_map/ppermute | solution.py:17
  97.6 1.6 collective-permute-done.7
  99.3 1.3 collective-permute-start.8
  100.6 4.7 %collective-permute-start.9 = (f32[6,18,1,128]{3,2,1,0:T(1,128)S(1)}, f32[6,18,1,128]{3,2,1,0:T(1,128)S(1)}, u32[]{:S(2)}, u32[]{:S(2)}) collective-permute-start(f32[6,18,1,128]{3,2,1,0:T(1,128)S(1)} %get-tuple-element.30), channel_id=1, source_target_pairs={{0,2},{1,3},{4,6},{5,7},{8,10},{9,11},{12,14},{13,15},{16,18},{17,... | collective-permute-start | bytes 165896 | tf_op jit(solution)/shard_map/ppermute | solution.py:17
  105.4 1.0 convert_element_type.15
  106.3 0.6 collective-permute-done.9
  107.0 0.6 copy-done.13
  108.2 1.6 copy.48
  109.8 1.4 collective-permute-start.10
  111.2 0.9 copy.50
  112.2 3.7 %collective-permute-start.11 = (f32[6,18,18,1]{2,1,3,0:T(8,128)S(1)}, f32[6,18,18,1]{2,1,3,0:T(8,128)}, u32[]{:S(2)}, u32[]{:S(2)}) collective-permute-start(f32[6,18,18,1]{2,1,3,0:T(8,128)S(1)} %copy.50), channel_id=1, source_target_pairs={{0,1},{2,3},{4,5},{6,7},{8,9},{10,11},{12,13},{14,15},{16,17},{18,... | collective-permute-start | bytes 23336 | tf_op jit(solution)/shard_map/ppermute | solution.py:17
  115.8 1.7 pad_maximum_fusion.4
  117.6 0.8 copy.49
  118.4 1.7 copy.51
  120.0 3.6 %pad_maximum_fusion.1 = (f32[6,18,18,129]{3,2,1,0:T(8,128)S(1)}, f32[6,18,18,129]{3,2,1,0:T(8,128)S(1)}) fusion(f32[6,18,18,1]{3,2,1,0:T(8,128)S(1)} %copy.49, f32[6,18,1,128]{3,2,1,0:T(1,128)} %copy-done.10, f32[6,1,16,128]{3,2,1,0:T(8,128)S(1)} %collective-permute-done.6, f32[3,16,16,128]{3,2,1,0:T(8,128)S(1)} %divide_add_fusion.2, ...), kind=kLoop, calls=%fused_computation.3 | loop fusion | flops 3009312 | bytes 3017088 | tf_op jit(solution)/shard_map/concatenate | solution.py:19
  123.7 2.3 %add_add_fusion = (f32[6,16,16,128]{3,2,1,0:T(8,128)}, f32[6,16,16,128]{3,2,1,0:T(8,128)}, f32[6,16,16,128]{3,2,1,0:T(8,128)}, f32[6,16,16,128]{3,2,1,0:T(8,128)}, f32[6]{0:T(128)S(1)}) fusion(f32[3,16,16,128]{3,2,1,0:T(8,128)S(1)} %divide_add_fusion.2, f32[3,16,16,128]{3,2,1,0:T(8,128)S(1)} %get-tuple-element.11, f32[6,18,17,128]{3,2,1,0:T(8,128)S(1)} %copy-done.19, ...), kind=kLoop, calls=%fused_computation.36 | loop fusion | flops 3145722 | bytes 7307288 | tf_op jit(solution)/shard_map/add | solution.py:43
  126.0 6.3 %psum.37 = f32[6]{0:T(128)S(1)} all-reduce(f32[6]{0:T(128)S(1)} %get-tuple-element.36), channel_id=1, replica_groups=mesh['freq'=2,'gx'=4,'gy'=2,'col'=2] {'gy','col'}, use_global_device_ids=true, to_apply=%region_5.6 | all-reduce | flops 6 | bytes 48 | tf_op jit(solution)/shard_map/psum | solution.py:121
  132.3 10.7 %psum.38 = f32[6]{0:T(128)S(1)} all-reduce(f32[6]{0:T(128)S(1)} %psum.37), channel_id=1, replica_groups=mesh['freq'=2,'gx'=4,'gy'=2,'col'=2] {'gx'}, use_global_device_ids=true, to_apply=%region_6.7 | all-reduce | flops 6 | bytes 48 | tf_op jit(solution)/shard_map/psum | solution.py:121
  143.1 1.6 fusion.53
  144.7 1.3 fusion.35
  146.0 1.3 fusion.47
  147.3 1.3 fusion.29
  148.6 1.6 fusion.41
  150.2 1.7 fusion.23
  152.0 0.7 subtract_reduce_fusion
  153.1 2.4 %psum.39 = f32[1,4,4]{2,1,0:T(4,128)S(1)} all-reduce(f32[1,4,4]{2,1,0:T(4,128)S(1)} %bitcast.39), channel_id=1, replica_groups=mesh['freq'=2,'gx'=4,'gy'=2,'col'=2] {'col'}, use_global_device_ids=true, to_apply=%region_10.11 | all-reduce | flops 16 | bytes 128 | tf_op jit(solution)/shard_map/psum | solution.py:163
  155.5 26.0 %all_gather.3 = f32[8,4,4]{2,1,0:T(4,128)S(1)} all-gather(f32[1,4,4]{2,1,0:T(4,128)S(1)} %psum.39), channel_id=1, replica_groups=mesh['freq'=2,'gx'=4,'gy'=2,'col'=2] {'gx','gy'}, dimensions={0}, use_global_device_ids=true | all-gather | bytes 576 | tf_op jit(solution)/shard_map/all_gather | solution.py:164
  181.6 0.7 div.40
  182.3 0.9 pad_maximum_fusion.13
  (101 shorter events, 3.2 us)
Async XLA Ops:
  0.6 31.0 %copy-start.32 = (bf16[16,16,128]{2,1,0:T(8,128)(2,1)S(1)}, bf16[16,16,128]{2,1,0:T(8,128)(2,1)}, u32[]{:S(2)}) copy-start(bf16[16,16,128]{2,1,0:T(8,128)(2,1)} %param.12) | copy-start | bytes 196612
  1.4 31.1 %collective-permute-start = (f32[6,1,16,128]{3,2,1,0:T(8,128)S(1)}, f32[6,1,16,128]{3,2,1,0:T(8,128)S(1)}, u32[]{:S(2)}, u32[]{:S(2)}) collective-permute-start(f32[6,1,16,128]{3,2,1,0:T(8,128)S(1)} %get-tuple-element.41), channel_id=1, source_target_pairs={{4,0},{8,4},{12,8},{5,1},{9,5},{13,9},{6,2},{10,6},{14,10},{7,3},{... | collective-permute-start | bytes 147464 | tf_op jit(solution)/shard_map/ppermute | solution.py:18
  2.7 29.8 %collective-permute-start.1 = (f32[6,1,16,128]{3,2,1,0:T(8,128)S(1)}, f32[6,1,16,128]{3,2,1,0:T(8,128)S(1)}, u32[]{:S(2)}, u32[]{:S(2)}) collective-permute-start(f32[6,1,16,128]{3,2,1,0:T(8,128)S(1)} %get-tuple-element.40), channel_id=1, source_target_pairs={{0,4},{4,8},{8,12},{1,5},{5,9},{9,13},{2,6},{6,10},{10,14},{3,7},{... | collective-permute-start | bytes 147464 | tf_op jit(solution)/shard_map/ppermute | solution.py:17
  12.9 19.5 %copy-start.33 = (s32[1,256]{1,0:T(1,128)S(1)}, s32[1,256]{1,0:T(1,128)}, u32[]{:S(2)}) copy-start(s32[1,256]{1,0:T(1,128)} %param.15) | copy-start | bytes 3076
  12.9 19.5 %copy-start.27 = (bf16[6,16,16,128]{3,2,1,0:T(8,128)(2,1)S(1)}, bf16[6,16,16,128]{3,2,1,0:T(8,128)(2,1)}, u32[]{:S(2)}) copy-start(bf16[6,16,16,128]{3,2,1,0:T(8,128)(2,1)} %param.10) | copy-start | bytes 1179652
  31.6 8.0 %copy-start.34 = (f32[2,3]{1,0:T(2,128)S(1)}, f32[2,3]{1,0:T(2,128)}, u32[]{:S(2)}) copy-start(f32[2,3]{1,0:T(2,128)} %param.16) | copy-start | bytes 76
  32.6 10.9 %collective-permute-start.2 = (f32[6,18,1,128]{3,2,1,0:T(1,128)S(1)}, f32[6,18,1,128]{3,2,1,0:T(1,128)}, u32[]{:S(2)}, u32[]{:S(2)}) collective-permute-start(f32[6,18,1,128]{3,2,1,0:T(1,128)S(1)} %get-tuple-element.35), channel_id=1, source_target_pairs={{2,0},{3,1},{6,4},{7,5},{10,8},{11,9},{14,12},{15,13},{18,16},{19,... | collective-permute-start | bytes 165896 | tf_op jit(solution)/shard_map/ppermute | solution.py:18
  33.9 9.6 %collective-permute-start.3 = (f32[6,18,1,128]{3,2,1,0:T(1,128)S(1)}, f32[6,18,1,128]{3,2,1,0:T(1,128)}, u32[]{:S(2)}, u32[]{:S(2)}) collective-permute-start(f32[6,18,1,128]{3,2,1,0:T(1,128)S(1)} %get-tuple-element.34), channel_id=1, source_target_pairs={{0,2},{1,3},{4,6},{5,7},{8,10},{9,11},{12,14},{13,15},{16,18},{17,... | collective-permute-start | bytes 165896 | tf_op jit(solution)/shard_map/ppermute | solution.py:17
  46.6 8.5 %collective-permute-start.4 = (f32[6,18,18,1]{2,1,3,0:T(8,128)}, f32[6,18,18,1]{2,1,3,0:T(8,128)S(1)}, u32[]{:S(2)}, u32[]{:S(2)}) collective-permute-start(f32[6,18,18,1]{2,1,3,0:T(8,128)} %copy.44), channel_id=1, source_target_pairs={{1,0},{3,2},{5,4},{7,6},{9,8},{11,10},{13,12},{15,14},{17,16},{19,... | collective-permute-start | bytes 23336 | tf_op jit(solution)/shard_map/ppermute | solution.py:18
  48.8 7.0 %collective-permute-start.5 = (f32[6,18,18,1]{2,1,3,0:T(8,128)S(1)}, f32[6,18,18,1]{2,1,3,0:T(8,128)}, u32[]{:S(2)}, u32[]{:S(2)}) collective-permute-start(f32[6,18,18,1]{2,1,3,0:T(8,128)S(1)} %copy.46), channel_id=1, source_target_pairs={{0,1},{2,3},{4,5},{6,7},{8,9},{10,11},{12,13},{14,15},{16,17},{18,... | collective-permute-start | bytes 23336 | tf_op jit(solution)/shard_map/ppermute | solution.py:17
  57.5 3.1 %copy-start.6 = (f32[32768]{0:T(1024)S(1)}, f32[32768]{0:T(1024)}, u32[]{:S(2)}) copy-start(f32[32768]{0:T(1024)} %scatter_custom_fusion) | copy-start | bytes 393220
  57.5 3.1 %copy-start.16 = (f32[6,18,17,128]{3,2,1,0:T(8,128)S(1)}, f32[6,18,17,128]{3,2,1,0:T(8,128)}, u32[]{:S(2)}) copy-start(f32[6,18,17,128]{3,2,1,0:T(8,128)} %get-tuple-element.32) | copy-start | bytes 2820100
  57.5 3.1 %copy-start.17 = (f32[6,18,17,128]{3,2,1,0:T(8,128)S(1)}, f32[6,18,17,128]{3,2,1,0:T(8,128)}, u32[]{:S(2)}) copy-start(f32[6,18,17,128]{3,2,1,0:T(8,128)} %get-tuple-element.33) | copy-start | bytes 2820100
  57.5 3.1 %copy-start.28 = (bf16[6,16,16,128]{3,2,1,0:T(8,128)(2,1)S(1)}, bf16[6,16,16,128]{3,2,1,0:T(8,128)(2,1)}, u32[]{:S(2)}) copy-start(bf16[6,16,16,128]{3,2,1,0:T(8,128)(2,1)} %param.10) | copy-start | bytes 1179652
  81.1 1.6 copy-start
  81.1 1.7 copy-start.20
  82.7 6.1 %copy-start.2 = (f32[1,16,16,128]{3,2,1,0:T(8,128)}, f32[1,16,16,128]{3,2,1,0:T(8,128)S(1)}, u32[]{:S(2)}) copy-start(f32[1,16,16,128]{3,2,1,0:T(8,128)S(1)} %get-tuple-element.15) | copy-start | bytes 393220
  88.8 1.8 copy-start.4
  88.8 1.8 copy-start.7
  88.9 1.8 copy-start.23
  88.9 1.8 copy-start.25
  88.9 1.8 copy-start.29
  91.5 13.9 %copy-start.31 = (bf16[6,16,16,128]{3,2,1,0:T(8,128)(2,1)S(1)}, bf16[6,16,16,128]{3,2,1,0:T(8,128)(2,1)}, u32[]{:S(2)}) copy-start(bf16[6,16,16,128]{3,2,1,0:T(8,128)(2,1)} %param.11) | copy-start | bytes 1179652
  91.5 6.1 %collective-permute-start.6 = (f32[6,1,16,128]{3,2,1,0:T(8,128)S(1)}, f32[6,1,16,128]{3,2,1,0:T(8,128)S(1)}, u32[]{:S(2)}, u32[]{:S(2)}) collective-permute-start(f32[6,1,16,128]{3,2,1,0:T(8,128)S(1)} %get-tuple-element.38), channel_id=1, source_target_pairs={{4,0},{8,4},{12,8},{5,1},{9,5},{13,9},{6,2},{10,6},{14,10},{7,3},{... | collective-permute-start | bytes 147464 | tf_op jit(solution)/shard_map/ppermute | solution.py:18
  93.0 6.3 %collective-permute-start.7 = (f32[6,1,16,128]{3,2,1,0:T(8,128)S(1)}, f32[6,1,16,128]{3,2,1,0:T(8,128)S(1)}, u32[]{:S(2)}, u32[]{:S(2)}) collective-permute-start(f32[6,1,16,128]{3,2,1,0:T(8,128)S(1)} %get-tuple-element.37), channel_id=1, source_target_pairs={{0,4},{4,8},{8,12},{1,5},{5,9},{9,13},{2,6},{6,10},{10,14},{3,7},{... | collective-permute-start | bytes 147464 | tf_op jit(solution)/shard_map/ppermute | solution.py:17
  99.3 7.0 %collective-permute-start.8 = (f32[6,18,1,128]{3,2,1,0:T(1,128)S(1)}, f32[6,18,1,128]{3,2,1,0:T(1,128)S(1)}, u32[]{:S(2)}, u32[]{:S(2)}) collective-permute-start(f32[6,18,1,128]{3,2,1,0:T(1,128)S(1)} %get-tuple-element.31), channel_id=1, source_target_pairs={{2,0},{3,1},{6,4},{7,5},{10,8},{11,9},{14,12},{15,13},{18,16},{19,... | collective-permute-start | bytes 165896 | tf_op jit(solution)/shard_map/ppermute | solution.py:18
  100.6 6.3 %collective-permute-start.9 = (f32[6,18,1,128]{3,2,1,0:T(1,128)S(1)}, f32[6,18,1,128]{3,2,1,0:T(1,128)S(1)}, u32[]{:S(2)}, u32[]{:S(2)}) collective-permute-start(f32[6,18,1,128]{3,2,1,0:T(1,128)S(1)} %get-tuple-element.30), channel_id=1, source_target_pairs={{0,2},{1,3},{4,6},{5,7},{8,10},{9,11},{12,14},{13,15},{16,18},{17,... | collective-permute-start | bytes 165896 | tf_op jit(solution)/shard_map/ppermute | solution.py:17
  106.3 0.6 copy-start.10
  107.0 0.6 copy-start.13
  109.8 6.0 %copy-start.11 = (f32[6,18,1,128]{3,2,1,0:T(1,128)S(1)}, f32[6,18,1,128]{3,2,1,0:T(1,128)}, u32[]{:S(2)}) copy-start(f32[6,18,1,128]{3,2,1,0:T(1,128)} %copy-done.10) | copy-start | bytes 165892
  109.8 6.0 %copy-start.14 = (f32[6,18,1,128]{3,2,1,0:T(1,128)S(1)}, f32[6,18,1,128]{3,2,1,0:T(1,128)}, u32[]{:S(2)}) copy-start(f32[6,18,1,128]{3,2,1,0:T(1,128)} %copy-done.13) | copy-start | bytes 165892
  109.8 7.8 %collective-permute-start.10 = (f32[6,18,18,1]{2,1,3,0:T(8,128)}, f32[6,18,18,1]{2,1,3,0:T(8,128)S(1)}, u32[]{:S(2)}, u32[]{:S(2)}) collective-permute-start(f32[6,18,18,1]{2,1,3,0:T(8,128)} %copy.48), channel_id=1, source_target_pairs={{1,0},{3,2},{5,4},{7,6},{9,8},{11,10},{13,12},{15,14},{17,16},{19,... | collective-permute-start | bytes 23336 | tf_op jit(solution)/shard_map/ppermute | solution.py:18
  112.2 6.2 %collective-permute-start.11 = (f32[6,18,18,1]{2,1,3,0:T(8,128)S(1)}, f32[6,18,18,1]{2,1,3,0:T(8,128)}, u32[]{:S(2)}, u32[]{:S(2)}) collective-permute-start(f32[6,18,18,1]{2,1,3,0:T(8,128)S(1)} %copy.50), channel_id=1, source_target_pairs={{0,1},{2,3},{4,5},{6,7},{8,9},{10,11},{12,13},{14,15},{16,17},{18,... | collective-permute-start | bytes 23336 | tf_op jit(solution)/shard_map/ppermute | solution.py:17
  120.0 3.7 %copy-start.8 = (f32[32768]{0:T(1024)S(1)}, f32[32768]{0:T(1024)}, u32[]{:S(2)}) copy-start(f32[32768]{0:T(1024)} %scatter_custom_fusion) | copy-start | bytes 393220
  120.0 3.7 %copy-start.18 = (f32[6,18,17,128]{3,2,1,0:T(8,128)S(1)}, f32[6,18,17,128]{3,2,1,0:T(8,128)}, u32[]{:S(2)}) copy-start(f32[6,18,17,128]{3,2,1,0:T(8,128)} %get-tuple-element.28) | copy-start | bytes 2820100
  120.0 3.7 %copy-start.19 = (f32[6,18,17,128]{3,2,1,0:T(8,128)S(1)}, f32[6,18,17,128]{3,2,1,0:T(8,128)}, u32[]{:S(2)}) copy-start(f32[6,18,17,128]{3,2,1,0:T(8,128)} %get-tuple-element.29) | copy-start | bytes 2820100
  143.1 1.6 copy-start.1
  143.1 1.6 copy-start.3
  143.1 1.6 copy-start.12
  143.1 1.6 copy-start.15
  143.1 1.6 copy-start.22
  150.2 1.8 copy-start.5
  150.2 1.8 copy-start.9
  150.2 1.8 copy-start.21
  150.2 1.8 copy-start.24
  150.2 1.8 copy-start.26
  150.2 1.8 copy-start.30
